TPU v7x, 32 devices: a whole 2x2x4 slice. The times are simulated.
32 devices in a mesh: groups: 2 (over y), head: 8 (over z, x), req: 2 (over core).
Axes of the slice: x: 2, y: 2, z: 4, core: 2. Of those that a mesh axis runs over, the one named last changes fastest.
Arguments:
- tokens: bfloat16 [2, 64, 2048], P('req', ('groups', 'head')), parts along dimension 1, may hold values from -4 to 4
- ssm_state: bfloat16 [2, 8, 128, 64, 128], P('req', 'groups', 'head'), parts along dimension 1, may hold values from -2 to 2
- conv_x_state: bfloat16 [2, 8, 3, 8192], P('req', 'groups', None, 'head'), parts along dimension 1, may hold values from -6 to 6
- conv_bc_state: bfloat16 [2, 8, 3, 2048], P('req', 'groups', None, 'head'), parts along dimension 1, may hold values from -6 to 6
- expert_ids: int32 [2, 64, 2], P('req', ('groups', 'head')), parts along dimension 1, may hold values from 0 to 7, all different within a row; in each aligned block of 4 rows (0 to 3, 4 to 7, ..., all dimensions but the last counted through in order) at most 2 rows name the same one
- mixer_gain: float32 [2048], replicated, may hold values from 0.5 to 1.5
- weight_xz: bfloat16 [2048, 16384], P(None, 'head'), may hold values from -0.125 to 0.125
- weight_bc: bfloat16 [2048, 2048], P(None, 'head'), may hold values from -0.125 to 0.125
- weight_delta: bfloat16 [2048, 128], P(None, 'head'), may hold values from -0.125 to 0.125
- delta_bias: float32 [128], P('head'), may hold values from -4 to -1
- decay_log: float32 [128], P('head'), may hold values from 0 to 2.8
- skip_gain: float32 [128], P('head'), may hold values from 0.5 to 1.5
- conv_x_kernel: float32 [4, 8192], P(None, 'head'), may hold values from -3 to 3
- conv_x_bias: float32 [8192], P('head'), may hold values from -3 to 3
- conv_bc_kernel: float32 [4, 2048], P(None, 'head'), may hold values from -3 to 3
- conv_bc_bias: float32 [2048], P('head'), may hold values from -3 to 3
- gated_gain: float32 [8192], P('head'), may hold values from 0.5 to 1.5
- weight_out: bfloat16 [8192, 2048], P('head'), may hold values from -0.0625 to 0.0625
- ffn_gain: float32 [2048], replicated, may hold values from 0.5 to 1.5
- router_weight: bfloat16 [2048, 8], replicated, may hold values from -0.125 to 0.125
- weight_up: bfloat16 [2048, 16384], P(None, 'head'), may hold values from -0.125 to 0.125
- weight_down: bfloat16 [16384, 2048], P('head'), may hold values from -0.125 to 0.125
Outputs:
- layer_out: bfloat16 [2, 64, 2048], P('req', ('groups', 'head')), parts along dimension 1
- new_state: bfloat16 [2, 8, 128, 64, 128], P('req', 'groups', 'head'), parts along dimension 1
- new_conv_x: bfloat16 [2, 8, 3, 8192], P('req', 'groups', None, 'head'), parts along dimension 1
- new_conv_bc: bfloat16 [2, 8, 3, 2048], P('req', 'groups', None, 'head'), parts along dimension 1
There are 2 independent parts, one for each index of `groups`. A program takes and returns all parts, laid end to end along the dimension named above; an argument that names none is the same for every part. Nothing has to cross between parts.
Inputs may be any that keep to these rules, and one draw needn't show every extreme that they name: `expert_ids`: each row names 2 different experts; in each aligned block of 4 rows no expert is named more than 2 times, and the bound is reached.
All inputs are finite; a program needn't handle non-finite values.
Results may differ from a plain program's by a relative error of at most 0.017.
Values may be sent and summed in bfloat16 or wider, within the bound.
No kernel may reach another device: no remote copies, remote signals or barrier semaphores. Data moves between devices by JAX's collectives and lax.ppermute only.
A program may use at most 128 MiB of HBM per device.

v0:
```python
import jax
import jax.numpy as jnp
from jax import lax
from jax.sharding import PartitionSpec as P

HEADS = 128
G = 8
EXPERTS = 8
TOP = 2
STEPS = 8
CAP = 2
eps = 1e-05
highest = lax.Precision.HIGHEST


def norm_rows(values, gain):
    mean_square = jnp.mean(values * values, axis=-1, keepdims=True)
    return values * lax.rsqrt(mean_square + eps) * gain


def causal_conv(past_rows, fresh_rows, kernel, offset):
    window = jnp.concatenate([past_rows, fresh_rows], axis=1)
    window_wide = window.astype(jnp.float32)
    fresh_count = fresh_rows.shape[1]
    running = offset + kernel[0] * window_wide[:, 0:fresh_count]
    for tap_index in range(1, kernel.shape[0]):
        running = running + kernel[tap_index] * window_wide[:, tap_index : tap_index + fresh_count]
    return (jax.nn.silu(running), window[:, fresh_count:])


def route_share(ffn_in, router_weight, chosen_ids):
    logits = jnp.dot(ffn_in, router_weight, preferred_element_type=jnp.float32)
    match_table = (chosen_ids[:, :, None] == jnp.arange(EXPERTS)[None, None, :]).astype(jnp.float32)
    picked = jnp.einsum("mke,me->mk", match_table, logits, precision=highest)
    first_weight = jax.nn.sigmoid(picked[:, 0] - picked[:, 1])
    return jnp.stack([first_weight, 1.0 - first_weight], axis=1)


def expert_hidden(rows_in, weight_up):
    return jnp.square(
        jnp.maximum(jnp.dot(rows_in, weight_up, preferred_element_type=jnp.float32), 0.0)
    ).astype(jnp.bfloat16)


def shards(
    tokens,
    ssm_state,
    conv_x_state,
    conv_bc_state,
    expert_ids,
    mixer_gain,
    weight_xz,
    weight_bc,
    weight_delta,
    delta_bias,
    decay_log,
    skip_gain,
    conv_x_kernel,
    conv_x_bias,
    conv_bc_kernel,
    conv_bc_bias,
    gated_gain,
    weight_out,
    ffn_gain,
    router_weight,
    weight_up,
    weight_down,
):
    head_count = lax.axis_size("head")
    my_index = lax.axis_index("head")
    tok_local = tokens.shape[1]
    width = tokens.shape[2]
    requests = ssm_state.shape[1]
    heads_local = ssm_state.shape[2]
    head_dim = ssm_state.shape[3]
    state_dim = ssm_state.shape[4]
    gathered = lax.all_gather(tokens, "head", axis=1, tiled=True)
    inputs = gathered.reshape(requests * STEPS, width)
    normed = norm_rows(inputs.astype(jnp.float32), mixer_gain).astype(jnp.bfloat16)
    proj_xz = jnp.dot(normed, weight_xz, preferred_element_type=jnp.float32).reshape(
        requests, STEPS, heads_local, 2, head_dim
    )
    x_fresh = (
        proj_xz[:, :, :, 0, :].reshape(requests, STEPS, heads_local * head_dim).astype(jnp.bfloat16)
    )
    z_gate = proj_xz[:, :, :, 1, :]
    bc_fresh = (
        jnp.dot(normed, weight_bc, preferred_element_type=jnp.float32)
        .reshape(requests, STEPS, -1)
        .astype(jnp.bfloat16)
    )
    delta = jax.nn.softplus(
        jnp.dot(normed, weight_delta, preferred_element_type=jnp.float32).reshape(
            requests, STEPS, heads_local
        )
        + delta_bias
    )
    x_conv, conv_x_new = causal_conv(conv_x_state[0], x_fresh, conv_x_kernel, conv_x_bias)
    bc_conv, conv_bc_new = causal_conv(conv_bc_state[0], bc_fresh, conv_bc_kernel, conv_bc_bias)
    bc_conv = bc_conv.astype(jnp.bfloat16)
    bc_all = lax.all_gather(bc_conv, "head", axis=2, tiled=True)
    bc_list = [bc_all[:, step_index] for step_index in range(STEPS)]
    head_global = my_index * heads_local + jnp.arange(heads_local)
    group_pick = (head_global[:, None] // (HEADS // G) == jnp.arange(G)[None, :]).astype(
        jnp.float32
    )
    x_heads = x_conv.reshape(requests, STEPS, heads_local, head_dim)
    decay_rate = jnp.exp(delta * -jnp.exp(decay_log))
    ssm_now = ssm_state[0]
    readings = []
    for step_index in range(STEPS):
        bc_values = bc_list[step_index].astype(jnp.float32).reshape(requests, 2, G, state_dim)
        b_heads = jnp.einsum("rgn,hg->rhn", bc_values[:, 0], group_pick, precision=highest)
        c_heads = jnp.einsum("rgn,hg->rhn", bc_values[:, 1], group_pick, precision=highest)
        x_step = x_heads[:, step_index]
        fresh_state = (
            decay_rate[:, step_index, :, None, None] * ssm_now.astype(jnp.float32)
            + (delta[:, step_index, :, None] * x_step)[..., None] * b_heads[:, :, None, :]
        )
        readings.append(
            jnp.einsum("rhpn,rhn->rhp", fresh_state, c_heads, precision=highest)
            + skip_gain[:, None] * x_step
        )
        ssm_now = fresh_state.astype(jnp.bfloat16)
    gated_out = jnp.stack(readings, axis=1) * jax.nn.silu(z_gate)
    group_normed = (
        norm_rows(gated_out, gated_gain.reshape(heads_local, head_dim))
        .astype(jnp.bfloat16)
        .reshape(requests * STEPS, heads_local * head_dim)
    )
    per_expert = head_count // EXPERTS
    mixer_out = lax.psum_scatter(
        jnp.dot(group_normed, weight_out, preferred_element_type=jnp.float32),
        "head",
        scatter_dimension=0,
        tiled=True,
    )
    residual = (tokens[0].astype(jnp.float32) + mixer_out).astype(jnp.bfloat16)
    ffn_in = norm_rows(residual.astype(jnp.float32), ffn_gain).astype(jnp.bfloat16)
    share = route_share(ffn_in, router_weight, expert_ids[0])
    chosen = expert_ids[0].reshape(-1)
    onehot = (chosen[:, None] == jnp.arange(EXPERTS)[None, :]).astype(jnp.int32)
    earlier = jnp.cumsum(onehot, axis=0) - onehot
    position = jnp.sum(earlier * onehot, axis=1)
    slot_index = chosen * CAP + position
    place = (jnp.arange(EXPERTS * CAP)[:, None] == slot_index[None, :]).astype(jnp.bfloat16)
    routed_rows = jnp.repeat(ffn_in, TOP, axis=0)
    packed = jnp.dot(place, routed_rows, preferred_element_type=jnp.float32).astype(jnp.bfloat16)
    outgoing = jnp.repeat(packed.reshape(EXPERTS, CAP, width), per_expert, axis=0)
    received = lax.all_to_all(outgoing, "head", split_axis=0, concat_axis=0, tiled=True)
    flat_rows = received.reshape(-1, width)
    hidden = expert_hidden(flat_rows, weight_up)
    computed = jnp.dot(hidden, weight_down, preferred_element_type=jnp.float32).reshape(
        received.shape[0], received.shape[1], width
    )
    returned = lax.all_to_all(
        computed.astype(jnp.bfloat16), "head", split_axis=0, concat_axis=0, tiled=True
    ).astype(computed.dtype)
    summed = (
        returned.reshape(EXPERTS, per_expert, CAP, width).sum(axis=1).reshape(EXPERTS * CAP, width)
    )
    per_route = jnp.dot(place.astype(jnp.float32).T, summed, precision=highest).reshape(
        tok_local, TOP, width
    )
    combined = jnp.sum(share[:, :, None] * per_route, axis=1)
    layer_out = (residual.astype(jnp.float32) + combined).astype(jnp.bfloat16)
    return (layer_out[None], ssm_now[None], conv_x_new[None], conv_bc_new[None])


def solution(mesh):
    return jax.shard_map(
        shards,
        mesh=mesh,
        in_specs=(
            P("req", ("groups", "head"), None),
            P("req", "groups", "head", None, None),
            P("req", "groups", None, "head"),
            P("req", "groups", None, "head"),
            P("req", ("groups", "head"), None),
            P(),
            P(None, "head"),
            P(None, "head"),
            P(None, "head"),
            P("head"),
            P("head"),
            P("head"),
            P(None, "head"),
            P("head"),
            P(None, "head"),
            P("head"),
            P("head"),
            P("head", None),
            P(),
            P(),
            P(None, "head"),
            P("head", None),
        ),
        out_specs=(
            P("req", ("groups", "head"), None),
            P("req", "groups", "head", None, None),
            P("req", "groups", None, "head"),
            P("req", "groups", None, "head"),
        ),
        check_vma=False,
    )
```

profile of v0, /device:TPU:0, one launch (start us, length us, event | category | flops | bytes accessed | tf_op | source)
XLA Modules:
  0.0 269.9 jit_solution(17759373759885222538)
XLA Ops:
  8.1 32.5 %all_gather.6 = bf16[1,32,2048]{2,0,1:T(2,128)(2,1)S(1)} all-gather(bf16[1,4,2048]{2,0,1:T(2,128)(2,1)S(1)} %copy.187), channel_id=1, replica_groups=mesh['groups'=2,'head'=8,'req'=2] {'head'}, dimensions={1}, use_global_device_ids=true | all-gather | bytes 147456 | tf_op jit(solution)/shard_map/all_gather | solution.py:77
  41.6 0.8 fusion.167
  42.4 1.0 convolution_convert_fusion.2
  44.2 30.5 %all_gather.7 = bf16[4,8,2048]{2,1,0:T(8,128)(2,1)S(1)} all-gather(bf16[4,8,256]{2,1,0:T(8,128)(2,1)S(1)} %multiply_convert_fusion.2), channel_id=1, replica_groups=mesh['groups'=2,'head'=8,'req'=2] {'head'}, dimensions={2}, use_global_device_ids=true | all-gather | bytes 147456 | tf_op jit(solution)/shard_map/all_gather | solution.py:101
  85.6 12.4 %copy.190 = bf16[2048,2048]{0,1:T(8,128)(2,1)} copy(bf16[2048,2048]{1,0:T(8,128)(2,1)} %param.28) | data formatting | bytes 16777216 | tf_op args[6]
  98.0 7.2 %fusion.74 = f32[4,8,16,2,64]{4,1,3,2,0:T(8,128)S(1)} fusion(bf16[16,2,64,2048,1]{3,2,1,0,4:T(8,128)(2,1)} %bitcast.433, bf16[1,32,2048]{2,1,0:T(8,128)(2,1)S(1)} %get-tuple-element.41, f32[2048]{0:T(1024)S(1)} %copy-done.31, f32[32]{0:T(128)S(1)} %add_rsqrt_fusion.2), kind=kOutput, calls=%fused_computation.102 | convolution fusion | flops 268697600 | bytes 8790144 | tf_op jit(solution)/shard_map/dot_general | solution.py:80
  106.7 4.3 %fusion.24 = f32[4,16,1,64]{3,2,1,0:T(1,128)S(1)} fusion(f32[4,16,128,1]{2,3,1,0:T(1,128)} %bitcast.467, bf16[1,4,16,64,128]{4,3,2,1,0:T(8,128)(2,1)S(1)} %copy-done.1, f32[4,16,128]{2,1,0:T(8,128)S(1)} %convolution_bitcast_fusion.7, f32[4,16,64]{2,1,0:T(8,128)S(1)} %get-tuple-element.57, f32[4,16]{1,0:T(4,128)S(1)} %bitcast.496), kind=kOutput, calls=%fused_computation.43 | convolution fusion | flops 8388608 | bytes 1147136 | tf_op jit(solution)/shard_map/rhpn,rhn->rhp/dot_general | solution.py:121
  111.0 5.0 %fusion.22 = f32[4,16,1,64]{3,2,1,0:T(1,128)S(1)} fusion(f32[4,16,128,1]{2,3,1,0:T(1,128)} %bitcast.468, f32[4,16,128]{2,1,0:T(8,128)S(1)} %convolution_bitcast_fusion.6, f32[4,16,64]{2,1,0:T(8,128)S(1)} %get-tuple-element.56, f32[4,16]{1,0:T(4,128)S(1)} %bitcast.491, bf16[1,4,16,64,128]{4,3,2,1,0:T(8,128)(2,1)S(1)} %copy-done.1, ...), kind=kOutput, calls=%fused_computation.41 | convolution fusion | flops 11010048 | bytes 1196544 | tf_op jit(solution)/shard_map/rhpn,rhn->rhp/dot_general | solution.py:121
  116.0 5.3 %fusion.20 = f32[4,16,1,64]{3,2,1,0:T(1,128)S(1)} fusion(f32[4,16,128,1]{2,3,1,0:T(1,128)S(1)} %bitcast.469, f32[4,16,128]{2,1,0:T(8,128)S(1)} %convolution_bitcast_fusion.5, f32[4,16,64]{2,1,0:T(8,128)S(1)} %get-tuple-element.55, f32[4,16]{1,0:T(4,128)S(1)} %bitcast.487, f32[4,16,128]{2,1,0:T(8,128)S(1)} %convolution_bitcast_fusion.6, ...), kind=kOutput, calls=%fused_computation.38 | convolution fusion | flops 13631488 | bytes 1245952 | tf_op jit(solution)/shard_map/rhpn,rhn->rhp/dot_general | solution.py:121
  121.3 3.2 %fusion.17 = bf16[4,16,64,128]{3,2,1,0:T(8,128)(2,1)S(1)} fusion(f32[4,16,128]{2,1,0:T(8,128)S(1)} %convolution_bitcast_fusion.4, f32[4,16,64]{2,1,0:T(8,128)S(1)} %get-tuple-element.54, f32[4,16]{1,0:T(4,128)S(1)} %bitcast.484, f32[4,16,128]{2,1,0:T(8,128)S(1)} %convolution_bitcast_fusion.5, f32[4,16,64]{2,1,0:T(8,128)S(1)} %get-tuple-element.55, ...), kind=kLoop, calls=%fused_computation.34 | loop fusion | flops 10485760 | bytes 2294784 | tf_op jit(solution)/shard_map/convert_element_type | solution.py:124
  124.6 6.9 %fusion.18 = f32[4,16,1,64]{3,2,1,0:T(1,128)S(1)} fusion(f32[4,16,128,1]{2,3,1,0:T(1,128)S(1)} %bitcast.470, f32[4,16,128]{2,1,0:T(8,128)S(1)} %convolution_bitcast_fusion.4, f32[4,16,64]{2,1,0:T(8,128)S(1)} %get-tuple-element.54, f32[4,16]{1,0:T(4,128)S(1)} %bitcast.485, f32[4,16,128]{2,1,0:T(8,128)S(1)} %convolution_bitcast_fusion.5, ...), kind=kOutput, calls=%fused_computation.35 | convolution fusion | flops 16252928 | bytes 1295360 | tf_op jit(solution)/shard_map/rhpn,rhn->rhp/dot_general | solution.py:121
  131.5 3.6 %fusion.16 = f32[4,16,1,64]{3,2,1,0:T(1,128)S(1)} fusion(f32[4,16,128,1]{2,3,1,0:T(1,128)S(1)} %bitcast.471, bf16[4,16,64,128]{3,2,1,0:T(8,128)(2,1)S(1)} %fusion.17, f32[4,16,128]{2,1,0:T(8,128)S(1)} %copy-done.6, f32[4,16,64]{2,1,0:T(8,128)S(1)} %get-tuple-element.53, f32[4,16]{1,0:T(4,128)S(1)} %bitcast.515), kind=kOutput, calls=%fused_computation.32 | convolution fusion | flops 8388608 | bytes 1147136 | tf_op jit(solution)/shard_map/rhpn,rhn->rhp/dot_general | solution.py:121
  135.1 4.7 %fusion.14 = f32[4,16,1,64]{3,2,1,0:T(1,128)S(1)} fusion(f32[4,16,128,1]{2,3,1,0:T(1,128)S(1)} %bitcast.472, f32[4,16,128]{2,1,0:T(8,128)S(1)} %copy-done.8, f32[4,16,64]{2,1,0:T(8,128)S(1)} %get-tuple-element.52, f32[4,16]{1,0:T(4,128)S(1)} %bitcast.511, bf16[4,16,64,128]{3,2,1,0:T(8,128)(2,1)S(1)} %fusion.17, f32[4,16,128]{2,1,0:T(8,128)S(1)} %copy-done.6, ...), kind=kOutput, calls=%fused_computation.29 | convolution fusion | flops 11010048 | bytes 1196544 | tf_op jit(solution)/shard_map/rhpn,rhn->rhp/dot_general | solution.py:121
  139.9 5.3 %fusion.12 = f32[4,16,1,64]{3,2,1,0:T(1,128)S(1)} fusion(f32[4,16,128,1]{2,3,1,0:T(1,128)S(1)} %bitcast.473, f32[4,16,128]{2,1,0:T(8,128)S(1)} %copy-done.10, f32[4,16,64]{2,1,0:T(8,128)S(1)} %get-tuple-element.51, f32[4,16]{1,0:T(4,128)S(1)} %bitcast.508, f32[4,16,128]{2,1,0:T(8,128)S(1)} %copy-done.8, f32[4,16,64]{2,1,0:T(8,128)S(1)} %get-tuple-element.52, ...), kind=kOutput, calls=%fused_computation.26 | convolution fusion | flops 13631488 | bytes 1245952 | tf_op jit(solution)/shard_map/rhpn,rhn->rhp/dot_general | solution.py:121
  145.3 6.7 %fusion.6 = f32[4,16,1,64]{3,2,1,0:T(1,128)S(1)} fusion(f32[4,16,128,1]{2,3,1,0:T(1,128)S(1)} %bitcast.474, f32[4,16,128]{2,1,0:T(8,128)S(1)} %copy-done.12, f32[4,16,64]{2,1,0:T(8,128)S(1)} %get-tuple-element.50, f32[4,16]{1,0:T(4,128)S(1)} %bitcast.506, f32[4,16,128]{2,1,0:T(8,128)S(1)} %copy-done.10, f32[4,16,64]{2,1,0:T(8,128)S(1)} %get-tuple-element.51, ...), kind=kOutput, calls=%fused_computation.19 | convolution fusion | flops 16252928 | bytes 1295360 | tf_op jit(solution)/shard_map/rhpn,rhn->rhp/dot_general | solution.py:121
  154.9 3.7 %fusion.84 = f32[32,2048]{1,0:T(8,128)} fusion(bf16[1024,2048]{1,0:T(8,128)(2,1)} %param.39, f32[32,1024]{1,0:T(8,128)S(1)} %mul.831, f32[32,1024]{1,0:T(8,128)S(1)} %stack.43, f32[32,1024]{1,0:T(8,128)S(1)} %squeeze.121, f32[1024]{0:T(1024)} %param.38), kind=kOutput, calls=%fused_computation.116 | convolution fusion | flops 134479872 | bytes 4853760 | tf_op jit(solution)/shard_map/dot_general | solution.py:133
  158.8 7.0 %add_convert_fusion = bf16[1,4,16,64,128]{4,3,2,1,0:T(8,128)(2,1)} fusion(bf16[1,4,16,64,128]{4,3,2,1,0:T(8,128)(2,1)S(1)} %copy-done.1, f32[4,16,128]{2,1,0:T(8,128)S(1)} %copy-done.13, f32[4,16,64]{2,1,0:T(8,128)S(1)} %get-tuple-element.50, f32[4,16,128]{2,1,0:T(8,128)S(1)} %copy-done.11, f32[4,16,64]{2,1,0:T(8,128)S(1)} %get-tuple-element.51, ...), kind=kLoop, calls=%fused_computation.12 | loop fusion | flops 20971520 | bytes 2492416 | tf_op jit(solution)/shard_map/convert_element_type | solution.py:124
  169.0 61.4 %all-reduce.3.cloned.1.call-done = f32[32,2048]{1,0:T(8,128)} async-done(((f32[32,2048]{1,0:T(8,128)}), f32[32,2048]{1,0:T(8,128)}) %all-reduce.3.cloned.1.call-update) | async-done | bytes 262160
  230.4 1.0 fusion.89
  232.5 3.9 %all-to-all-start = ((bf16[8,2,2048]{2,1,0:T(2,128)(2,1)}), bf16[8,2,2048]{2,1,0:T(2,128)(2,1)S(1)}, u32[]{:S(2)}, u32[]{:S(2)}) async-start(bf16[8,2,2048]{2,1,0:T(2,128)(2,1)} %reshape_broadcast_in_dim_reshape.3), calls=%async_computation | async-start | bytes 131072 | tf_op jit(solution)/shard_map/all_to_all | solution.py:150
  236.7 6.6 %all-to-all-done = bf16[8,2,2048]{2,1,0:T(2,128)(2,1)S(1)} async-done(((bf16[8,2,2048]{2,1,0:T(2,128)(2,1)}), bf16[8,2,2048]{2,1,0:T(2,128)(2,1)S(1)}, u32[]{:S(2)}, u32[]{:S(2)}) %all-to-all-start) | async-done | bytes 65568 | tf_op jit(solution)/shard_map/all_to_all | solution.py:150
  243.3 8.0 %convolution_convert_fusion.1 = bf16[16,2048]{1,0:T(8,128)(2,1)S(1)} fusion(bf16[2048,2048]{1,0:T(8,128)(2,1)} %param.43, bf16[16,2048]{1,0:T(8,128)(2,1)S(1)} %reshape.366, bf16[2048,2048]{1,0:T(8,128)(2,1)} %param.42), kind=kOutput, calls=%fused_computation.6 | convolution fusion | flops 268566528 | bytes 16908288 | tf_op jit(solution)/shard_map/dot_general | solution.py:153
  252.1 3.3 %all-to-all-start.1 = ((bf16[8,2,2048]{2,1,0:T(2,128)(2,1)}), bf16[8,2,2048]{2,1,0:T(2,128)(2,1)S(1)}, u32[]{:S(2)}, u32[]{:S(2)}) async-start(bf16[8,2,2048]{2,1,0:T(2,128)(2,1)} %convert_element_type.233), calls=%async_computation.1 | async-start | bytes 131072 | tf_op jit(solution)/shard_map/all_to_all | solution.py:156
  255.5 6.8 %all-to-all-done.1 = bf16[8,2,2048]{2,1,0:T(2,128)(2,1)S(1)} async-done(((bf16[8,2,2048]{2,1,0:T(2,128)(2,1)}), bf16[8,2,2048]{2,1,0:T(2,128)(2,1)S(1)}, u32[]{:S(2)}, u32[]{:S(2)}) %all-to-all-start.1) | async-done | bytes 65568 | tf_op jit(solution)/shard_map/all_to_all | solution.py:156
  (188 shorter events, 23.0 us)
Async XLA Ops:
  7.2 35.3 %copy-start = (bf16[2048,256]{1,0:T(8,128)(2,1)S(1)}, bf16[2048,256]{1,0:T(8,128)(2,1)}, u32[]{:S(2)}) copy-start(bf16[2048,256]{1,0:T(8,128)(2,1)} %param.29) | copy-start | bytes 3145732
  7.2 78.5 %copy-start.46 = (f32[16]{0:T(128)S(1)}, f32[16]{0:T(128)}, u32[]{:S(2)}) copy-start(f32[16]{0:T(128)} %param.32) | copy-start | bytes 196
  7.2 223.2 %all-reduce.3.cloned.1.call-start = ((), (), s32[]{:S(2)}) async-start(), calls=%async_computation.2 | async-start | bytes 524288
  85.6 12.4 %copy-start.31 = (f32[2048]{0:T(1024)S(1)}, f32[2048]{0:T(1024)}, u32[]{:S(2)}) copy-start(f32[2048]{0:T(1024)} %param.27) | copy-start | bytes 24580
  98.0 7.5 %copy-start.21 = (bf16[1,4,3,1024]{3,1,2,0:T(4,128)(2,1)S(1)}, bf16[1,4,3,1024]{3,1,2,0:T(4,128)(2,1)}, u32[]{:S(2)}) copy-start(bf16[1,4,3,1024]{3,1,2,0:T(4,128)(2,1)} %param.24) | copy-start | bytes 73732
  98.0 7.5 %copy-start.30 = (f32[4,1024]{1,0:T(4,128)S(1)}, f32[4,1024]{1,0:T(4,128)}, u32[]{:S(2)}) copy-start(f32[4,1024]{1,0:T(4,128)} %param.34) | copy-start | bytes 49156
  98.0 7.6 %copy-start.41 = (f32[1024]{0:T(1024)S(1)}, f32[1024]{0:T(1024)}, u32[]{:S(2)}) copy-start(f32[1024]{0:T(1024)} %param.35) | copy-start | bytes 12292
  106.4 18.1 %copy-start.22 = (f32[4,1,16]{2,1,0:T(1,128)}, f32[4,1,16]{2,1,0:T(1,128)S(1)}, u32[]{:S(2)}) copy-start(f32[4,1,16]{2,1,0:T(1,128)S(1)} %get-tuple-element.62) | copy-start | bytes 772
  106.4 18.1 %copy-start.24 = (f32[4,1,16]{2,1,0:T(1,128)}, f32[4,1,16]{2,1,0:T(1,128)S(1)}, u32[]{:S(2)}) copy-start(f32[4,1,16]{2,1,0:T(1,128)S(1)} %get-tuple-element.63) | copy-start | bytes 772
  106.4 18.1 %copy-start.26 = (f32[4,1,16]{2,1,0:T(1,128)}, f32[4,1,16]{2,1,0:T(1,128)S(1)}, u32[]{:S(2)}) copy-start(f32[4,1,16]{2,1,0:T(1,128)S(1)} %get-tuple-element.64) | copy-start | bytes 772
  106.4 18.1 %copy-start.28 = (f32[4,1,16]{2,1,0:T(1,128)}, f32[4,1,16]{2,1,0:T(1,128)S(1)}, u32[]{:S(2)}) copy-start(f32[4,1,16]{2,1,0:T(1,128)S(1)} %get-tuple-element.65) | copy-start | bytes 772
  106.5 38.7 %copy-start.32 = (f32[4,1,16]{2,1,0:T(1,128)}, f32[4,1,16]{2,1,0:T(1,128)S(1)}, u32[]{:S(2)}) copy-start(f32[4,1,16]{2,1,0:T(1,128)S(1)} %get-tuple-element.58) | copy-start | bytes 772
  106.5 38.7 %copy-start.34 = (f32[4,1,16]{2,1,0:T(1,128)}, f32[4,1,16]{2,1,0:T(1,128)S(1)}, u32[]{:S(2)}) copy-start(f32[4,1,16]{2,1,0:T(1,128)S(1)} %get-tuple-element.59) | copy-start | bytes 772
  106.5 38.7 %copy-start.36 = (f32[4,1,16]{2,1,0:T(1,128)}, f32[4,1,16]{2,1,0:T(1,128)S(1)}, u32[]{:S(2)}) copy-start(f32[4,1,16]{2,1,0:T(1,128)S(1)} %get-tuple-element.60) | copy-start | bytes 772
  106.5 38.7 %copy-start.38 = (f32[4,1,16]{2,1,0:T(1,128)}, f32[4,1,16]{2,1,0:T(1,128)S(1)}, u32[]{:S(2)}) copy-start(f32[4,1,16]{2,1,0:T(1,128)S(1)} %get-tuple-element.61) | copy-start | bytes 772
  106.6 38.6 %copy-start.2 = (f32[4,16,64]{2,1,0:T(8,128)}, f32[4,16,64]{2,1,0:T(8,128)S(1)}, u32[]{:S(2)}) copy-start(f32[4,16,64]{2,1,0:T(8,128)S(1)} %get-tuple-element.52) | copy-start | bytes 49156
  106.6 38.6 %copy-start.4 = (f32[4,16,64]{2,1,0:T(8,128)}, f32[4,16,64]{2,1,0:T(8,128)S(1)}, u32[]{:S(2)}) copy-start(f32[4,16,64]{2,1,0:T(8,128)S(1)} %get-tuple-element.53) | copy-start | bytes 49156
  158.6 7.2 %copy-start.42 = (s32[1,4,2]{1,2,0:T(2,128)S(1)}, s32[1,4,2]{1,2,0:T(2,128)}, u32[]{:S(2)}) copy-start(s32[1,4,2]{1,2,0:T(2,128)} %param.26) | copy-start | bytes 100
  158.6 9.1 %copy-start.48 = (u32[32]{0:T(128)S(1)}, u32[32]{0:T(128)}, u32[]{:S(2)}) copy-start(u32[32]{0:T(128)} %constant.62) | copy-start | bytes 388
  158.6 71.8 %copy-start.14 = (bf16[1,4,2048]{2,1,0:T(4,128)(2,1)S(1)}, bf16[1,4,2048]{2,1,0:T(4,128)(2,1)}, u32[]{:S(2)}) copy-start(bf16[1,4,2048]{2,1,0:T(4,128)(2,1)} %param.22) | copy-start | bytes 49156
  158.6 72.8 %copy-start.40 = (f32[2048]{0:T(1024)S(1)}, f32[2048]{0:T(1024)}, u32[]{:S(2)}) copy-start(f32[2048]{0:T(1024)} %param.40) | copy-start | bytes 24580
  158.6 72.9 %copy-start.45 = (bf16[2048,8]{0,1:T(8,128)(2,1)S(1)}, bf16[2048,8]{0,1:T(8,128)(2,1)}, u32[]{:S(2)}) copy-start(bf16[2048,8]{0,1:T(8,128)(2,1)} %param.41) | copy-start | bytes 98308
  232.5 10.8 %all-to-all-start = ((bf16[8,2,2048]{2,1,0:T(2,128)(2,1)}), bf16[8,2,2048]{2,1,0:T(2,128)(2,1)S(1)}, u32[]{:S(2)}, u32[]{:S(2)}) async-start(bf16[8,2,2048]{2,1,0:T(2,128)(2,1)} %reshape_broadcast_in_dim_reshape.3), calls=%async_computation | async-start | bytes 131072 | tf_op jit(solution)/shard_map/all_to_all | solution.py:150
  252.1 10.2 %all-to-all-start.1 = ((bf16[8,2,2048]{2,1,0:T(2,128)(2,1)}), bf16[8,2,2048]{2,1,0:T(2,128)(2,1)S(1)}, u32[]{:S(2)}, u32[]{:S(2)}) async-start(bf16[8,2,2048]{2,1,0:T(2,128)(2,1)} %convert_element_type.233), calls=%async_computation.1 | async-start | bytes 131072 | tf_op jit(solution)/shard_map/all_to_all | solution.py:156
  (28 other events, 114.1 us)
Sparse Core Ops, SparseCore 0:
  158.8 71.5 all-reduce.2
where the time goes:
time: 271 us; the launch traced here: 270 us
  waiting for transfers between devices  74.9 us (28%)
  matrix products  72.9 us (27%)
  blocking collectives  63 us (23%)
  local copies, waits for them, and re-layouts  21.8 us (8%)
  between operations  15.6 us (6%)
  other arithmetic  14.4 us (5%)
  starting transfers between devices  7.28 us (3%)
    unnamed x2, waiting for transfers between devices  61.4 us
    dot_general x8, matrix products, shards(): jnp.einsum('rhpn,rhn->rhp', fresh_state, c_heads, precision=highest)  41.8 us
    all_gather x1, blocking collectives, shards(): gathered = lax.all_gather(tokens, 'head', axis=1, tiled=True)  32.5 us
    all_gather x1, blocking collectives, shards(): bc_all = lax.all_gather(bc_conv, 'head', axis=2, tiled=True)  30.5 us
    unnamed x114, local copies, waits for them, and re-layouts  16.2 us
    convert_element_type x2, other arithmetic, shards(): ssm_now = fresh_state.astype(jnp.bfloat16)  10.2 us
    dot_general x1, matrix products, shards(): jnp.dot(hidden, weight_down, preferred_element_type=jnp.float32)  8.05 us
    dot_general x1, matrix products, shards(): jnp.dot(normed, weight_xz, preferred_element_type=jnp.float32)  7.21 us
  transfers between devices with their start and end apart: 3, of which 3 were waited for; matrix products, arithmetic and copies ran while one was open for 4% of the time, Pallas kernels for 0%

commit v1 on v0

--- a/solution.py
+++ b/solution.py
@@ -11,6 +11,16 @@
 CAP = 2
 eps = 1e-05
 highest = lax.Precision.HIGHEST
+
+
+def _follow_marks(panel, dimension_no):
+    panel = jnp.moveaxis(panel, 0, dimension_no)
+    formed = panel.shape
+    return panel.reshape(
+        *formed[:dimension_no],
+        formed[dimension_no] * formed[dimension_no + 1],
+        *formed[dimension_no + 2 :]
+    )
 
 
 def norm_rows(values, gain):
@@ -74,7 +84,27 @@
     heads_local = ssm_state.shape[2]
     head_dim = ssm_state.shape[3]
     state_dim = ssm_state.shape[4]
-    gathered = lax.all_gather(tokens, "head", axis=1, tiled=True)
+    n_shards = jax.lax.axis_size("head")
+    seen = [(m, (m + 1) % n_shards) for m in range(n_shards)]
+    buffer = [(j, u) for u, j in seen]
+    next_value, local_now = ([], [])
+    for kk in range(n_shards - 1):
+        if kk % 2 == 0:
+            next_value.append(
+                jax.lax.ppermute(
+                    next_value[-1] if next_value else tokens, perm=seen, axis_name="head"
+                )
+            )
+        else:
+            local_now.append(
+                jax.lax.ppermute(
+                    local_now[-1] if local_now else tokens, axis_name="head", perm=buffer
+                )
+            )
+    high = jnp.stack([*next_value[::-1], tokens, *local_now])
+    near = jax.lax.axis_index("head") - len(next_value)
+    high = high[(jnp.arange(n_shards) - near) % n_shards]
+    gathered = _follow_marks(high, 1)
     inputs = gathered.reshape(requests * STEPS, width)
     normed = norm_rows(inputs.astype(jnp.float32), mixer_gain).astype(jnp.bfloat16)
     proj_xz = jnp.dot(normed, weight_xz, preferred_element_type=jnp.float32).reshape(

time: 271 us -> 272 us (level)
  blocking collectives: 63 us -> 30.8 us
  waiting for transfers between devices: 74.9 us -> 93.8 us
  starting transfers between devices: 7.28 us -> 22.9 us
    all_gather x1 -> x0, blocking collectives: 32.5 us -> none  [shards(): gathered = lax.all_gather(tokens, 'head', axis=1, tiled=True)]
    ppermute x0 -> x7, starting transfers between devices: none -> 15.6 us  [the longest x3 12.6 us: shards(): jax.lax.ppermute(local_now[-1] if local_now else tokens, axis_name='head'...]
    unnamed x2, waiting for transfers between devices: 61.4 us -> 71 us
    ppermute x0 -> x7, waiting for transfers between devices: none -> 9.37 us  [the longest x4 8.07 us: shards(): jax.lax.ppermute(next_value[-1] if next_value else tokens, perm=seen, axi...]
    unnamed x114 -> x80, local copies, waits for them, and re-layouts: 16.2 us -> 15.2 us
  transfers between devices with their start and end apart: 3 -> 10, of which waited for: 3 -> 6; matrix products, arithmetic and copies ran while one was open for 4% -> 7% of each run, Pallas kernels for 0% -> 0%
where the time goes in v1:
time: 272 us
  waiting for transfers between devices  93.8 us (34%)
  matrix products  71.5 us (26%)
  blocking collectives  30.8 us (11%)
  starting transfers between devices  22.9 us (8%)
  local copies, waits for them, and re-layouts  22.8 us (8%)
  between operations  15.4 us (6%)
  other arithmetic  14.4 us (5%)
    unnamed x2, waiting for transfers between devices  71 us
    dot_general x8, matrix products, shards(): jnp.einsum('rhpn,rhn->rhp', fresh_state, c_heads, precision=highest)  41.4 us
    all_gather x1, blocking collectives, shards(): bc_all = lax.all_gather(bc_conv, 'head', axis=2, tiled=True)  30.8 us
    unnamed x80, local copies, waits for them, and re-layouts  15.2 us
    ppermute x3, starting transfers between devices, shards(): jax.lax.ppermute(local_now[-1] if local_now else tokens, axis_name='head'...  12.6 us
    convert_element_type x2, other arithmetic, shards(): ssm_now = fresh_state.astype(jnp.bfloat16)  10.2 us
    ppermute x4, waiting for transfers between devices, shards(): jax.lax.ppermute(next_value[-1] if next_value else tokens, perm=seen, axi...  8.07 us
    dot_general x1, matrix products, shards(): jnp.dot(hidden, weight_down, preferred_element_type=jnp.float32)  8.05 us
  transfers between devices with their start and end apart: 10, of which 6 were waited for; matrix products, arithmetic and copies ran while one was open for 7% of the time, Pallas kernels for 0%

profile of v1, /device:TPU:0, one launch (start us, length us, event | category | flops | bytes accessed | tf_op | source)
XLA Modules:
  0.0 271.6 jit_solution(6247793713937820430)
XLA Ops:
  10.2 3.1 %collective-permute-start.4 = (bf16[1,4,2048]{2,1,0:T(4,128)(2,1)}, bf16[1,4,2048]{2,1,0:T(4,128)(2,1)S(1)}, u32[]{:S(2)}, u32[]{:S(2)}) collective-permute-start(bf16[1,4,2048]{2,1,0:T(4,128)(2,1)} %param.22), channel_id=1, source_target_pairs={{2,0},{4,2},{6,4},{8,6},{10,8},{12,10},{14,12},{0,14},{3,1},{5,3},... | collective-permute-start | bytes 49160 | tf_op jit(solution)/shard_map/ppermute | solution.py:100
  17.5 6.4 %collective-permute-done.1 = bf16[1,4,2048]{2,1,0:T(4,128)(2,1)S(1)} collective-permute-done((bf16[1,4,2048]{2,1,0:T(4,128)(2,1)S(1)}, bf16[1,4,2048]{2,1,0:T(4,128)(2,1)S(1)}, u32[]{:S(2)}, u32[]{:S(2)}) %collective-permute-start.1) | collective-permute-done | bytes 16416 | tf_op jit(solution)/shard_map/ppermute | solution.py:94
  23.9 4.8 %collective-permute-start.5 = (bf16[1,4,2048]{2,1,0:T(4,128)(2,1)S(1)}, bf16[1,4,2048]{2,1,0:T(4,128)(2,1)S(1)}, u32[]{:S(2)}, u32[]{:S(2)}) collective-permute-start(bf16[1,4,2048]{2,1,0:T(4,128)(2,1)S(1)} %collective-permute-done.4), channel_id=1, source_target_pairs={{2,0},{4,2},{6,4},{8,6},{10,8},{12,10},{14,12},{0,14},{3,1},{5,3},... | collective-permute-start | bytes 49160 | tf_op jit(solution)/shard_map/ppermute | solution.py:100
  30.4 12.3 %copy.147 = bf16[2048,2048]{0,1:T(8,128)(2,1)} copy(bf16[2048,2048]{1,0:T(8,128)(2,1)} %param.28) | data formatting | bytes 16777216 | tf_op args[6]
  45.3 4.8 %collective-permute-start.6 = (bf16[1,4,2048]{2,1,0:T(4,128)(2,1)S(1)}, bf16[1,4,2048]{2,1,0:T(4,128)(2,1)S(1)}, u32[]{:S(2)}, u32[]{:S(2)}) collective-permute-start(bf16[1,4,2048]{2,1,0:T(4,128)(2,1)S(1)} %collective-permute-done.5), channel_id=1, source_target_pairs={{2,0},{4,2},{6,4},{8,6},{10,8},{12,10},{14,12},{0,14},{3,1},{5,3},... | collective-permute-start | bytes 49160 | tf_op jit(solution)/shard_map/ppermute | solution.py:100
  53.0 30.8 %all_gather.3 = bf16[4,8,2048]{2,1,0:T(8,128)(2,1)S(1)} all-gather(bf16[4,8,256]{2,1,0:T(8,128)(2,1)S(1)} %multiply_convert_fusion.3), channel_id=1, replica_groups=mesh['groups'=2,'head'=8,'req'=2] {'head'}, dimensions={2}, use_global_device_ids=true | all-gather | bytes 147456 | tf_op jit(solution)/shard_map/all_gather | solution.py:131
  93.6 7.2 %fusion.74 = f32[4,8,16,2,64]{4,1,3,2,0:T(8,128)S(1)} fusion(bf16[16,2,64,2048,1]{3,2,1,0,4:T(8,128)(2,1)} %bitcast.445, bf16[4,8,2048,1,1]{2,1,0,3,4:T(8,128)(2,1)S(1)} %reshape.465), kind=kOutput, calls=%fused_computation.108 | convolution fusion | flops 268435456 | bytes 8781824 | tf_op jit(solution)/shard_map/dot_general | solution.py:110
  102.8 4.3 %fusion.24 = f32[4,16,1,64]{3,2,1,0:T(1,128)S(1)} fusion(f32[4,16,128,1]{2,3,1,0:T(1,128)} %bitcast.480, bf16[1,4,16,64,128]{4,3,2,1,0:T(8,128)(2,1)S(1)} %copy-done.1, f32[4,16,128]{2,1,0:T(8,128)S(1)} %convolution_bitcast_fusion.7, f32[4,16,64]{2,1,0:T(8,128)S(1)} %get-tuple-element.51, f32[4,16]{1,0:T(4,128)S(1)} %bitcast.509), kind=kOutput, calls=%fused_computation.44 | convolution fusion | flops 8388608 | bytes 1147136 | tf_op jit(solution)/shard_map/rhpn,rhn->rhp/dot_general | solution.py:151
  107.1 4.9 %fusion.22 = f32[4,16,1,64]{3,2,1,0:T(1,128)S(1)} fusion(f32[4,16,128,1]{2,3,1,0:T(1,128)S(1)} %bitcast.482, f32[4,16,128]{2,1,0:T(8,128)S(1)} %convolution_bitcast_fusion.6, f32[4,16,64]{2,1,0:T(8,128)S(1)} %get-tuple-element.50, f32[4,16]{1,0:T(4,128)S(1)} %bitcast.504, bf16[1,4,16,64,128]{4,3,2,1,0:T(8,128)(2,1)S(1)} %copy-done.1, ...), kind=kOutput, calls=%fused_computation.42 | convolution fusion | flops 11010048 | bytes 1196544 | tf_op jit(solution)/shard_map/rhpn,rhn->rhp/dot_general | solution.py:151
  112.0 5.3 %fusion.20 = f32[4,16,1,64]{3,2,1,0:T(1,128)S(1)} fusion(f32[4,16,128,1]{2,3,1,0:T(1,128)S(1)} %bitcast.483, f32[4,16,128]{2,1,0:T(8,128)S(1)} %convolution_bitcast_fusion.5, f32[4,16,64]{2,1,0:T(8,128)S(1)} %get-tuple-element.49, f32[4,16]{1,0:T(4,128)S(1)} %bitcast.500, f32[4,16,128]{2,1,0:T(8,128)S(1)} %convolution_bitcast_fusion.6, ...), kind=kOutput, calls=%fused_computation.39 | convolution fusion | flops 13631488 | bytes 1245952 | tf_op jit(solution)/shard_map/rhpn,rhn->rhp/dot_general | solution.py:151
  117.3 3.2 %fusion.17 = bf16[4,16,64,128]{3,2,1,0:T(8,128)(2,1)S(1)} fusion(f32[4,16,128]{2,1,0:T(8,128)S(1)} %convolution_bitcast_fusion.4, f32[4,16,64]{2,1,0:T(8,128)S(1)} %get-tuple-element.48, f32[4,16]{1,0:T(4,128)S(1)} %bitcast.497, f32[4,16,128]{2,1,0:T(8,128)S(1)} %convolution_bitcast_fusion.5, f32[4,16,64]{2,1,0:T(8,128)S(1)} %get-tuple-element.49, ...), kind=kLoop, calls=%fused_computation.35 | loop fusion | flops 10485760 | bytes 2294784 | tf_op jit(solution)/shard_map/convert_element_type | solution.py:154
  120.5 6.7 %fusion.18 = f32[4,16,1,64]{3,2,1,0:T(1,128)S(1)} fusion(f32[4,16,128,1]{2,3,1,0:T(1,128)S(1)} %bitcast.484, f32[4,16,128]{2,1,0:T(8,128)S(1)} %convolution_bitcast_fusion.4, f32[4,16,64]{2,1,0:T(8,128)S(1)} %get-tuple-element.48, f32[4,16]{1,0:T(4,128)S(1)} %bitcast.498, f32[4,16,128]{2,1,0:T(8,128)S(1)} %convolution_bitcast_fusion.5, ...), kind=kOutput, calls=%fused_computation.36 | convolution fusion | flops 16252928 | bytes 1295360 | tf_op jit(solution)/shard_map/rhpn,rhn->rhp/dot_general | solution.py:151
  127.2 3.6 %fusion.16 = f32[4,16,1,64]{3,2,1,0:T(1,128)S(1)} fusion(f32[4,16,128,1]{2,3,1,0:T(1,128)S(1)} %bitcast.485, bf16[4,16,64,128]{3,2,1,0:T(8,128)(2,1)S(1)} %fusion.17, f32[4,16,128]{2,1,0:T(8,128)S(1)} %convolution_bitcast_fusion.3, f32[4,16,64]{2,1,0:T(8,128)S(1)} %get-tuple-element.47, f32[4,16]{1,0:T(4,128)S(1)} %bitcast.528), kind=kOutput, calls=%fused_computation.33 | convolution fusion | flops 8388608 | bytes 1147136 | tf_op jit(solution)/shard_map/rhpn,rhn->rhp/dot_general | solution.py:151
  130.8 4.7 %fusion.14 = f32[4,16,1,64]{3,2,1,0:T(1,128)S(1)} fusion(f32[4,16,128,1]{2,3,1,0:T(1,128)S(1)} %bitcast.486, f32[4,16,128]{2,1,0:T(8,128)S(1)} %convolution_bitcast_fusion.2, f32[4,16,64]{2,1,0:T(8,128)S(1)} %get-tuple-element.46, f32[4,16]{1,0:T(4,128)S(1)} %bitcast.524, bf16[4,16,64,128]{3,2,1,0:T(8,128)(2,1)S(1)} %fusion.17, ...), kind=kOutput, calls=%fused_computation.30 | convolution fusion | flops 11010048 | bytes 1196544 | tf_op jit(solution)/shard_map/rhpn,rhn->rhp/dot_general | solution.py:151
  135.5 5.3 %fusion.12 = f32[4,16,1,64]{3,2,1,0:T(1,128)S(1)} fusion(f32[4,16,128,1]{2,3,1,0:T(1,128)S(1)} %bitcast.487, f32[4,16,128]{2,1,0:T(8,128)S(1)} %copy-done.2, f32[4,16,64]{2,1,0:T(8,128)S(1)} %get-tuple-element.45, f32[4,16]{1,0:T(4,128)S(1)} %bitcast.521, f32[4,16,128]{2,1,0:T(8,128)S(1)} %convolution_bitcast_fusion.2, ...), kind=kOutput, calls=%fused_computation.27 | convolution fusion | flops 13631488 | bytes 1245952 | tf_op jit(solution)/shard_map/rhpn,rhn->rhp/dot_general | solution.py:151
  140.9 7.0 %add_convert_fusion = bf16[1,4,16,64,128]{4,3,2,1,0:T(8,128)(2,1)} fusion(bf16[1,4,16,64,128]{4,3,2,1,0:T(8,128)(2,1)S(1)} %copy-done.1, f32[4,16,128]{2,1,0:T(8,128)S(1)} %copy-done.3, f32[4,16,64]{2,1,0:T(8,128)S(1)} %get-tuple-element.44, f32[4,16,128]{2,1,0:T(8,128)S(1)} %copy-done.2, f32[4,16,64]{2,1,0:T(8,128)S(1)} %get-tuple-element.45, ...), kind=kLoop, calls=%fused_computation.13 | loop fusion | flops 20971520 | bytes 2492416 | tf_op jit(solution)/shard_map/convert_element_type | solution.py:154
  147.9 6.7 %fusion.6 = f32[4,16,1,64]{3,2,1,0:T(1,128)S(1)} fusion(f32[4,16,128,1]{2,3,1,0:T(1,128)S(1)} %bitcast.481, f32[4,16,128]{2,1,0:T(8,128)S(1)} %copy-done.3, f32[4,16,64]{2,1,0:T(8,128)S(1)} %get-tuple-element.44, f32[4,16]{1,0:T(4,128)S(1)} %bitcast.520, f32[4,16,128]{2,1,0:T(8,128)S(1)} %copy-done.2, f32[4,16,64]{2,1,0:T(8,128)S(1)} %get-tuple-element.45, ...), kind=kOutput, calls=%fused_computation.20 | convolution fusion | flops 16252928 | bytes 1295360 | tf_op jit(solution)/shard_map/rhpn,rhn->rhp/dot_general | solution.py:151
  156.1 3.7 %fusion.76 = f32[32,2048]{1,0:T(8,128)} fusion(bf16[1024,2048]{1,0:T(8,128)(2,1)} %param.39, f32[32,1024]{1,0:T(8,128)S(1)} %mul.853, f32[32,1024]{1,0:T(8,128)S(1)} %stack.79, f32[32,1024]{1,0:T(8,128)S(1)} %squeeze.121, f32[1024]{0:T(1024)S(1)} %copy-done.21), kind=kOutput, calls=%fused_computation.112 | convolution fusion | flops 134479872 | bytes 4853760 | tf_op jit(solution)/shard_map/dot_general | solution.py:163
  161.1 71.0 %all-reduce.3.cloned.1.call-done = f32[32,2048]{1,0:T(8,128)} async-done(((f32[32,2048]{1,0:T(8,128)}), f32[32,2048]{1,0:T(8,128)}) %all-reduce.3.cloned.1.call-update) | async-done | bytes 262160
  234.2 3.9 %all-to-all-start = ((bf16[8,2,2048]{2,1,0:T(2,128)(2,1)}), bf16[8,2,2048]{2,1,0:T(2,128)(2,1)S(1)}, u32[]{:S(2)}, u32[]{:S(2)}) async-start(bf16[8,2,2048]{2,1,0:T(2,128)(2,1)} %reshape_broadcast_in_dim_reshape.3), calls=%async_computation | async-start | bytes 131072 | tf_op jit(solution)/shard_map/all_to_all | solution.py:180
  238.4 6.6 %all-to-all-done = bf16[8,2,2048]{2,1,0:T(2,128)(2,1)S(1)} async-done(((bf16[8,2,2048]{2,1,0:T(2,128)(2,1)}), bf16[8,2,2048]{2,1,0:T(2,128)(2,1)S(1)}, u32[]{:S(2)}, u32[]{:S(2)}) %all-to-all-start) | async-done | bytes 65568 | tf_op jit(solution)/shard_map/all_to_all | solution.py:180
  245.0 8.0 %convolution_convert_fusion.1 = bf16[16,2048]{1,0:T(8,128)(2,1)S(1)} fusion(bf16[2048,2048]{1,0:T(8,128)(2,1)} %param.43, bf16[16,2048]{1,0:T(8,128)(2,1)S(1)} %reshape.446, bf16[2048,2048]{1,0:T(8,128)(2,1)} %param.42), kind=kOutput, calls=%fused_computation.7 | convolution fusion | flops 268566528 | bytes 16908288 | tf_op jit(solution)/shard_map/dot_general | solution.py:183
  253.7 3.3 %all-to-all-start.1 = ((bf16[8,2,2048]{2,1,0:T(2,128)(2,1)}), bf16[8,2,2048]{2,1,0:T(2,128)(2,1)S(1)}, u32[]{:S(2)}, u32[]{:S(2)}) async-start(bf16[8,2,2048]{2,1,0:T(2,128)(2,1)} %convert_element_type.253), calls=%async_computation.1 | async-start | bytes 131072 | tf_op jit(solution)/shard_map/all_to_all | solution.py:186
  257.1 6.8 %all-to-all-done.1 = bf16[8,2,2048]{2,1,0:T(2,128)(2,1)S(1)} async-done(((bf16[8,2,2048]{2,1,0:T(2,128)(2,1)}), bf16[8,2,2048]{2,1,0:T(2,128)(2,1)S(1)}, u32[]{:S(2)}, u32[]{:S(2)}) %all-to-all-start.1) | async-done | bytes 65568 | tf_op jit(solution)/shard_map/all_to_all | solution.py:186
  (174 shorter events, 31.8 us)
Async XLA Ops:
  7.2 45.4 %copy-start = (bf16[2048,256]{1,0:T(8,128)(2,1)S(1)}, bf16[2048,256]{1,0:T(8,128)(2,1)}, u32[]{:S(2)}) copy-start(bf16[2048,256]{1,0:T(8,128)(2,1)} %param.29) | copy-start | bytes 3145732
  7.2 224.9 %all-reduce.3.cloned.1.call-start = ((), (), s32[]{:S(2)}) async-start(), calls=%async_computation.2 | async-start | bytes 524288
  7.2 10.2 %collective-permute-start = (bf16[1,4,2048]{2,1,0:T(4,128)(2,1)}, bf16[1,4,2048]{2,1,0:T(4,128)(2,1)S(1)}, u32[]{:S(2)}, u32[]{:S(2)}) collective-permute-start(bf16[1,4,2048]{2,1,0:T(4,128)(2,1)} %param.22), channel_id=1, source_target_pairs={{0,2},{2,4},{4,6},{6,8},{8,10},{10,12},{12,14},{14,0},{1,3},{3,5},... | collective-permute-start | bytes 49160 | tf_op jit(solution)/shard_map/ppermute | solution.py:94
  10.2 13.7 %collective-permute-start.4 = (bf16[1,4,2048]{2,1,0:T(4,128)(2,1)}, bf16[1,4,2048]{2,1,0:T(4,128)(2,1)S(1)}, u32[]{:S(2)}, u32[]{:S(2)}) collective-permute-start(bf16[1,4,2048]{2,1,0:T(4,128)(2,1)} %param.22), channel_id=1, source_target_pairs={{2,0},{4,2},{6,4},{8,6},{10,8},{12,10},{14,12},{0,14},{3,1},{5,3},... | collective-permute-start | bytes 49160 | tf_op jit(solution)/shard_map/ppermute | solution.py:100
  16.2 14.2 %copy-start.24 = (s32[8]{0:T(128)}, s32[8]{0:T(128)S(1)}, u32[]{:S(2)}) copy-start(s32[8]{0:T(128)S(1)} %multiply_add_fusion.20) | copy-start | bytes 100
  17.5 6.4 %collective-permute-start.1 = (bf16[1,4,2048]{2,1,0:T(4,128)(2,1)S(1)}, bf16[1,4,2048]{2,1,0:T(4,128)(2,1)S(1)}, u32[]{:S(2)}, u32[]{:S(2)}) collective-permute-start(bf16[1,4,2048]{2,1,0:T(4,128)(2,1)S(1)} %collective-permute-done), channel_id=1, source_target_pairs={{0,2},{2,4},{4,6},{6,8},{8,10},{10,12},{12,14},{14,0},{1,3},{3,5},... | collective-permute-start | bytes 49160 | tf_op jit(solution)/shard_map/ppermute | solution.py:94
  23.9 6.4 %collective-permute-start.2 = (bf16[1,4,2048]{2,1,0:T(4,128)(2,1)S(1)}, bf16[1,4,2048]{2,1,0:T(4,128)(2,1)S(1)}, u32[]{:S(2)}, u32[]{:S(2)}) collective-permute-start(bf16[1,4,2048]{2,1,0:T(4,128)(2,1)S(1)} %collective-permute-done.1), channel_id=1, source_target_pairs={{0,2},{2,4},{4,6},{6,8},{8,10},{10,12},{12,14},{14,0},{1,3},{3,5},... | collective-permute-start | bytes 49160 | tf_op jit(solution)/shard_map/ppermute | solution.py:94
  23.9 21.4 %collective-permute-start.5 = (bf16[1,4,2048]{2,1,0:T(4,128)(2,1)S(1)}, bf16[1,4,2048]{2,1,0:T(4,128)(2,1)S(1)}, u32[]{:S(2)}, u32[]{:S(2)}) collective-permute-start(bf16[1,4,2048]{2,1,0:T(4,128)(2,1)S(1)} %collective-permute-done.4), channel_id=1, source_target_pairs={{2,0},{4,2},{6,4},{8,6},{10,8},{12,10},{14,12},{0,14},{3,1},{5,3},... | collective-permute-start | bytes 49160 | tf_op jit(solution)/shard_map/ppermute | solution.py:100
  30.3 19.7 %collective-permute-start.3 = (bf16[1,4,2048]{2,1,0:T(4,128)(2,1)S(1)}, bf16[1,4,2048]{2,1,0:T(4,128)(2,1)S(1)}, u32[]{:S(2)}, u32[]{:S(2)}) collective-permute-start(bf16[1,4,2048]{2,1,0:T(4,128)(2,1)S(1)} %collective-permute-done.2), channel_id=1, source_target_pairs={{0,2},{2,4},{4,6},{6,8},{8,10},{10,12},{12,14},{14,0},{1,3},{3,5},... | collective-permute-start | bytes 49160 | tf_op jit(solution)/shard_map/ppermute | solution.py:94
  30.4 12.4 %copy-start.14 = (bf16[1,4,3,1024]{3,1,2,0:T(4,128)(2,1)S(1)}, bf16[1,4,3,1024]{3,1,2,0:T(4,128)(2,1)}, u32[]{:S(2)}) copy-start(bf16[1,4,3,1024]{3,1,2,0:T(4,128)(2,1)} %param.24) | copy-start | bytes 73732
  30.4 12.4 %copy-start.17 = (bf16[1,4,3,256]{3,1,2,0:T(4,128)(2,1)S(1)}, bf16[1,4,3,256]{3,1,2,0:T(4,128)(2,1)}, u32[]{:S(2)}) copy-start(bf16[1,4,3,256]{3,1,2,0:T(4,128)(2,1)} %param.25) | copy-start | bytes 18436
  30.4 12.4 %copy-start.20 = (s32[1,4,2]{1,2,0:T(2,128)S(1)}, s32[1,4,2]{1,2,0:T(2,128)}, u32[]{:S(2)}) copy-start(s32[1,4,2]{1,2,0:T(2,128)} %param.26) | copy-start | bytes 100
  30.4 13.6 %copy-start.28 = (u32[32]{0:T(128)S(1)}, u32[32]{0:T(128)}, u32[]{:S(2)}) copy-start(u32[32]{0:T(128)} %constant.81) | copy-start | bytes 388
  30.4 19.7 %copy-start.5 = (bf16[1,4,2048]{2,1,0:T(4,128)(2,1)S(1)}, bf16[1,4,2048]{2,1,0:T(4,128)(2,1)}, u32[]{:S(2)}) copy-start(bf16[1,4,2048]{2,1,0:T(4,128)(2,1)} %param.22) | copy-start | bytes 49156
  30.4 22.0 %copy-start.4 = (f32[2048]{0:T(1024)S(1)}, f32[2048]{0:T(1024)}, u32[]{:S(2)}) copy-start(f32[2048]{0:T(1024)} %param.27) | copy-start | bytes 24580
  45.3 6.2 %collective-permute-start.6 = (bf16[1,4,2048]{2,1,0:T(4,128)(2,1)S(1)}, bf16[1,4,2048]{2,1,0:T(4,128)(2,1)S(1)}, u32[]{:S(2)}, u32[]{:S(2)}) collective-permute-start(bf16[1,4,2048]{2,1,0:T(4,128)(2,1)S(1)} %collective-permute-done.5), channel_id=1, source_target_pairs={{2,0},{4,2},{6,4},{8,6},{10,8},{12,10},{14,12},{0,14},{3,1},{5,3},... | collective-permute-start | bytes 49160 | tf_op jit(solution)/shard_map/ppermute | solution.py:100
  156.0 76.1 %copy-start.6 = (bf16[1,4,2048]{2,1,0:T(4,128)(2,1)S(1)}, bf16[1,4,2048]{2,1,0:T(4,128)(2,1)}, u32[]{:S(2)}) copy-start(bf16[1,4,2048]{2,1,0:T(4,128)(2,1)} %param.22) | copy-start | bytes 49156
  156.0 77.0 %copy-start.16 = (f32[2048]{0:T(1024)S(1)}, f32[2048]{0:T(1024)}, u32[]{:S(2)}) copy-start(f32[2048]{0:T(1024)} %param.40) | copy-start | bytes 24580
  156.0 77.1 %copy-start.27 = (bf16[2048,8]{0,1:T(8,128)(2,1)S(1)}, bf16[2048,8]{0,1:T(8,128)(2,1)}, u32[]{:S(2)}) copy-start(bf16[2048,8]{0,1:T(8,128)(2,1)} %param.41) | copy-start | bytes 98308
  156.1 77.3 %copy-start.25 = (s32[8]{0:T(128)S(1)}, s32[8]{0:T(128)}, u32[]{:S(2)}) copy-start(s32[8]{0:T(128)} %copy-done.24) | copy-start | bytes 100
  156.1 82.0 %copy-start.22 = (s32[4,2]{1,0:T(4,128)S(1)}, s32[4,2]{1,0:T(4,128)}, u32[]{:S(2)}) copy-start(s32[4,2]{1,0:T(4,128)} %copy.177) | copy-start | bytes 100
  234.2 10.8 %all-to-all-start = ((bf16[8,2,2048]{2,1,0:T(2,128)(2,1)}), bf16[8,2,2048]{2,1,0:T(2,128)(2,1)S(1)}, u32[]{:S(2)}, u32[]{:S(2)}) async-start(bf16[8,2,2048]{2,1,0:T(2,128)(2,1)} %reshape_broadcast_in_dim_reshape.3), calls=%async_computation | async-start | bytes 131072 | tf_op jit(solution)/shard_map/all_to_all | solution.py:180
  245.0 19.0 %copy-start.18 = (pred[4,2,16]{2,1,0:T(4,128)(4,1)S(1)}, pred[4,2,16]{2,1,0:T(4,128)(4,1)}, u32[]{:S(2)}) copy-start(pred[4,2,16]{2,1,0:T(4,128)(4,1)} %eq.84) | copy-start | bytes 388
  253.7 10.2 %all-to-all-start.1 = ((bf16[8,2,2048]{2,1,0:T(2,128)(2,1)}), bf16[8,2,2048]{2,1,0:T(2,128)(2,1)S(1)}, u32[]{:S(2)}, u32[]{:S(2)}) async-start(bf16[8,2,2048]{2,1,0:T(2,128)(2,1)} %convert_element_type.253), calls=%async_computation.1 | async-start | bytes 131072 | tf_op jit(solution)/shard_map/all_to_all | solution.py:186
  (15 other events, 74.2 us)
Sparse Core Ops, SparseCore 0:
  159.9 72.1 all-reduce.2
